TPU v7x, 512 devices: a whole 4x4x16 slice. The times are simulated.
512 devices in a mesh: dp: 4 (over x), ctx: 16 (over z), mp: 8 (over y, core).
Axes of the slice: x: 4, y: 4, z: 16, core: 2. Of those that a mesh axis runs over, the one named last changes fastest.
Arguments:
- tokens: bfloat16 [4, 2048, 4096], P('dp', 'ctx'), may hold values from -52 to 52
- x_weight: bfloat16 [4096, 8192], P(('dp', 'ctx'), 'mp'), may hold values from -0.09375 to 0.09375
- bc_weight: bfloat16 [4096, 1024], P(('dp', 'ctx'), 'mp'), may hold values from -0.09375 to 0.09375
- dt_weight: bfloat16 [4096, 128], P(('dp', 'ctx'), 'mp'), may hold values from -0.0234375 to 0.0234375
- conv_x: float32 [5, 8192], P(None, 'mp'), may hold values from -0.5 to 0.5
- conv_bc: float32 [5, 1024], P(None, 'mp'), may hold values from -0.5 to 0.5
- dt_bias: float32 [128], P('mp'), may hold values from -4.5 to -2.5
- a_log: float32 [128], P('mp')
- d_skip: float32 [128], P('mp'), may hold values from 0.5 to 1.5
- norm_gain: float32 [8192], P('mp'), may hold values from 0.5 to 1.5
Outputs:
- mixer_out: bfloat16 [4, 2048, 8192], P('dp', 'ctx', 'mp')
- kurtosis: float32 [4096], P('mp')
All inputs are finite; a program needn't handle non-finite values.
Results may differ from a plain program's by a relative error of at most 0.015.
Values may be sent and summed in bfloat16 or wider, within the bound.
No kernel may reach another device: no remote copies, remote signals or barrier semaphores. Data moves between devices by JAX's collectives and lax.ppermute only.
A program may use at most 64 MiB of HBM per device.

v0:
```python
import jax
import jax.numpy as jnp
from jax import lax
from jax.sharding import PartitionSpec as P

ROOT = 64
HEADS = 128
G = 4
NS = 128
HIGH = lax.Precision.HIGHEST


def passed_along(value, axis, steps):
    count = lax.axis_size(axis)
    first, last = (max(0, -steps), min(count, count - steps))
    return lax.ppermute(value, axis, [(source, source + steps) for source in range(first, last)])


def entering(array, axis, combine, identity):
    length, place = (lax.axis_size(axis), lax.axis_index(axis))
    everything = jax.tree.map(
        lambda part, kind: lax.all_gather(part.astype(kind), axis),
        array,
        (jnp.bfloat16, jnp.bfloat16),
    )
    start = jax.tree.map(
        lambda part, zero: jnp.broadcast_to(jnp.asarray(zero, part.dtype), part.shape),
        array,
        identity,
    )

    def step(k, before):
        reached = k < place
        new = combine(
            before, jax.tree.map(lambda part, own: part[k].astype(own.dtype), everything, array)
        )
        return jax.tree.map(lambda a, b: jnp.where(reached, a, b), new, before)

    return lax.fori_loop(0, length, step, start)


def hadamard_signs(sign_order):
    row_index = lax.broadcasted_iota(jnp.int32, (sign_order, sign_order), 0)
    col_index = lax.broadcasted_iota(jnp.int32, (sign_order, sign_order), 1)
    common = jnp.bitwise_and(row_index, col_index)
    parity = jnp.zeros((sign_order, sign_order), jnp.int32)
    for bit_index in range(sign_order.bit_length() - 1):
        parity = parity + jnp.bitwise_and(jnp.right_shift(common, bit_index), 1)
    return 1.0 - 2.0 * jnp.bitwise_and(parity, 1).astype(jnp.float32)


def kurtosis_from(powers, row_count):
    average = powers[0] / row_count
    second = powers[1] / row_count - average * average
    fourth = (
        powers[3] / row_count
        - 4.0 * average * powers[2] / row_count
        + 6.0 * average * average * powers[1] / row_count
        - 3.0 * average * average * average * average
    )
    return fourth / (second * second + 1e-06)


def chain_states(earlier, later):
    return (earlier[0] * later[0], later[0][:, :, None, None] * earlier[1] + later[1])


def shards(
    tokens, x_weight, bc_weight, dt_weight, conv_x, conv_bc, dt_bias, a_log, d_skip, norm_gain
):
    tok_rows = tokens.shape[1]
    model_width = tokens.shape[2]
    signs = hadamard_signs(ROOT)
    blocks = tokens.reshape(tok_rows, ROOT, ROOT)
    first_pass = jnp.einsum(
        "tab,ac->tcb", blocks, signs.astype(jnp.bfloat16), preferred_element_type=jnp.float32
    )
    second = jnp.einsum("tcb,bd->tcd", first_pass, signs, precision=HIGH)
    rotated = (second.reshape(tok_rows, model_width) / ROOT).astype(jnp.bfloat16)
    channel_share = model_width // lax.axis_size("mp")
    own_cols = lax.dynamic_slice_in_dim(
        rotated, lax.axis_index("mp") * channel_share, channel_share, 1
    ).astype(jnp.float32)
    square = own_cols * own_cols
    powers = jnp.stack(
        [
            jnp.sum(own_cols, 0),
            jnp.sum(square, 0),
            jnp.sum(square * own_cols, 0),
            jnp.sum(square * square, 0),
        ]
    )
    row_count = float(tok_rows * lax.axis_size("dp") * lax.axis_size("ctx"))
    totals = lax.psum(powers, ("dp", "ctx"))
    kurtosis = kurtosis_from(totals, row_count)
    panels = (
        lax.all_gather(x_weight, ("dp", "ctx"), axis=0, tiled=True),
        lax.all_gather(bc_weight, ("dp", "ctx"), axis=0, tiled=True),
        lax.all_gather(dt_weight, ("dp", "ctx"), axis=0, tiled=True),
    )
    projected = tuple(
        (jnp.dot(rotated, panel, preferred_element_type=jnp.float32) for panel in panels)
    )
    x_cols = x_weight.shape[1]
    joined = jnp.concatenate(
        [projected[0].astype(jnp.bfloat16), projected[1].astype(jnp.bfloat16)], 1
    )
    dt_proj = lax.optimization_barrier(projected[2].astype(jnp.bfloat16))
    conv_taps = jnp.concatenate([conv_x, conv_bc], 1)
    kernel = conv_taps.shape[0] - 1
    rim_rows = passed_along(joined[tok_rows - (kernel - 1) :], "ctx", 1)
    padded = jnp.concatenate([rim_rows, joined], 0)
    conv_sum = conv_taps[kernel]
    for tap_index in range(kernel):
        conv_sum = conv_sum + conv_taps[tap_index] * padded[tap_index : tap_index + tok_rows]
    convolved = jax.nn.silu(conv_sum).astype(jnp.bfloat16)
    x_conv = convolved[:, :x_cols]
    group_all = lax.all_gather(convolved[:, x_cols:], "mp", axis=1, tiled=True)
    heads_dev = dt_weight.shape[1]
    head_size = x_cols // heads_dev
    per_group = HEADS // G
    groups_here = max(1, heads_dev // per_group)
    heads_local = heads_dev // groups_here
    first_group = lax.axis_index("mp") * heads_dev // per_group
    write_all = group_all[:, : G * NS].reshape(tok_rows, G, NS)
    read_all = group_all[:, G * NS :].reshape(tok_rows, G, NS)
    write_here = lax.dynamic_slice_in_dim(write_all, first_group, groups_here, 1)
    read_here = lax.dynamic_slice_in_dim(read_all, first_group, groups_here, 1)
    step_size = jax.nn.softplus(dt_proj.astype(jnp.float32) + dt_bias)
    decay_rate = step_size * jnp.exp(a_log)
    cumulative = jnp.cumsum(decay_rate, 0)
    block_end = cumulative[-1]
    causal = lax.broadcasted_iota(jnp.int32, (tok_rows, tok_rows), 0) >= lax.broadcasted_iota(
        jnp.int32, (tok_rows, tok_rows), 1
    )
    spread = cumulative.T[:, :, None] - cumulative.T[:, None, :]
    decay_mask = jnp.where(causal, jnp.exp(-jnp.where(causal, spread, 0.0)), 0.0)
    scores = jnp.einsum("tgn,sgn->gts", read_here, write_here, preferred_element_type=jnp.float32)
    weights = (
        scores[:, None]
        * decay_mask.reshape(groups_here, heads_local, tok_rows, tok_rows)
        * step_size.T.reshape(groups_here, heads_local, 1, tok_rows)
    ).astype(jnp.bfloat16)
    x_heads = x_conv.reshape(tok_rows, groups_here, heads_local, head_size)
    within_block = jnp.einsum(
        "ghts,sghp->tghp", weights, x_heads, preferred_element_type=jnp.float32
    )
    update = (
        (jnp.exp(-(block_end - cumulative)) * step_size).reshape(
            tok_rows, groups_here, heads_local
        )[..., None]
        * x_heads
    ).astype(jnp.bfloat16)
    contrib = jnp.einsum("sghp,sgn->ghpn", update, write_here, preferred_element_type=jnp.float32)
    identity = (jnp.ones((groups_here, heads_local), jnp.float32), jnp.zeros_like(contrib))
    carried = entering(
        (jnp.exp(-block_end).reshape(groups_here, heads_local), contrib),
        "ctx",
        chain_states,
        identity,
    )
    from_before = jnp.exp(-cumulative).reshape(tok_rows, groups_here, heads_local)[
        ..., None
    ] * jnp.einsum("tgn,ghpn->tghp", read_here.astype(jnp.float32), carried[1], precision=HIGH)
    output_raw = (
        within_block
        + from_before
        + d_skip.reshape(groups_here, heads_local)[None, :, :, None] * x_heads.astype(jnp.float32)
    )
    mean_square = jnp.mean(output_raw * output_raw, -1, keepdims=True)
    normed = (
        output_raw
        * lax.rsqrt(mean_square + 1e-05)
        * norm_gain.reshape(groups_here, heads_local, head_size)
    )
    return (normed.reshape(1, tok_rows, x_cols).astype(jnp.bfloat16), kurtosis)


def solution(mesh):
    return jax.shard_map(
        shards,
        mesh=mesh,
        in_specs=(
            P("dp", "ctx", None),
            P(("dp", "ctx"), "mp"),
            P(("dp", "ctx"), "mp"),
            P(("dp", "ctx"), "mp"),
            P(None, "mp"),
            P(None, "mp"),
            P("mp"),
            P("mp"),
            P("mp"),
            P("mp"),
        ),
        out_specs=(P("dp", "ctx", "mp"), P("mp")),
        check_vma=False,
    )
```

profile of v0, /device:TPU:8, one launch (start us, length us, event | category | flops | bytes accessed | tf_op | source)
XLA Modules:
  0.0 532.6 jit_solution(13258673937758941600)
XLA Ops:
  7.2 0.0 all-gather.10.cloned.1.call-start
  7.2 0.7 all-gather.10.cloned.1.call-update
  7.9 0.0 all-gather.8.cloned.1.call-start
  8.0 0.7 all-gather.8.cloned.1.call-update
  8.7 0.0 all-gather.12.cloned.1.call-start
  8.7 1.6 copy.40
  10.3 88.7 %all-gather.2 = bf16[64,64,16]{1,2,0:T(8,128)(2,1)S(1)} all-gather(bf16[1,64,16]{1,2,0:T(8,128)(2,1)S(1)} %bitcast.105), channel_id=1, replica_groups=mesh['dp'=4,'ctx'=16,'mp'=8] {'dp','ctx'}, dimensions={0}, use_global_device_ids=true | all-gather | bytes 133120 | tf_op jit(solution)/shard_map/all_gather | solution.py:99
  99.1 0.1 copy.47
  99.1 0.3 reshape.184
  99.4 0.9 convolution_bitcast_fusion
  100.4 3.3 multiply_convert_fusion
  103.7 0.3 convolution_convert_fusion.3
  104.0 0.1 broadcast_multiply_fusion
  104.0 0.1 copy.48
  104.2 0.2 reduce_window_sum.11
  104.3 0.1 copy.52
  104.4 0.1 fusion.54
  104.5 49.7 %all-gather.10.cloned.1.call-done = bf16[4096,128]{1,0:T(8,128)(2,1)} async-done(((bf16[64,128]{1,0:T(8,128)(2,1)}), bf16[4096,128]{1,0:T(8,128)(2,1)}) %all-gather.10.cloned.1.call-update) | async-done | bytes 1048592 | tf_op jit(solution)/shard_map/all_gather | solution.py:98
  154.2 1.7 convolution_convert_fusion.2
  155.9 154.7 %all-gather.8.cloned.1.call-done = bf16[4096,1024]{1,0:T(8,128)(2,1)} async-done(((bf16[64,1024]{1,0:T(8,128)(2,1)}), bf16[4096,1024]{1,0:T(8,128)(2,1)}) %all-gather.8.cloned.1.call-update) | async-done | bytes 8388624 | tf_op jit(solution)/shard_map/all_gather | solution.py:97
  310.6 4.7 convolution_convert_fusion.1
  315.3 3.7 collective-permute-start
  319.0 0.1 slice_reduce_fusion.4
  319.1 0.2 copy.53
  319.3 1.0 collective-permute-done
  320.4 0.1 maximum_maximum_fusion
  320.4 0.4 multiply_convert_fusion.2
  320.9 11.9 %all_gather.26 = bf16[128,1024]{1,0:T(8,128)(2,1)S(1)} all-gather(bf16[128,128]{1,0:T(8,128)(2,1)S(1)} %slice.84), channel_id=1, replica_groups=mesh['dp'=4,'ctx'=16,'mp'=8] {'mp'}, dimensions={1}, use_global_device_ids=true | all-gather | bytes 294912 | tf_op jit(solution)/shard_map/all_gather | solution.py:118
  332.9 0.2 copy.54
  333.1 0.1 constant_dynamic-slice_fusion
  333.2 0.9 convolution_convert_fusion
  334.2 0.1 copy.51
  334.2 0.1 copy.49
  334.3 0.1 mul.262
  334.3 28.7 %all-gather.3 = bf16[16,1,16]{2,1,0:T(2,128)(2,1)S(1)} all-gather(bf16[1,1,16]{2,1,0:T(2,128)(2,1)S(1)} %get-tuple-element.160), channel_id=2, replica_groups=mesh['dp'=4,'ctx'=16,'mp'=8] {'ctx'}, dimensions={0}, use_global_device_ids=true | all-gather | bytes 544 | tf_op jit(solution)/shard_map/all_gather | solution.py:22
  363.0 0.3 convert_reduce_fusion
  363.4 141.2 %psum.7 = f32[4,512]{1,0:T(4,128)S(1)} all-reduce(f32[4,512]{1,0:T(4,128)S(1)} %pad_maximum_fusion.1), channel_id=1, replica_groups=mesh['dp'=4,'ctx'=16,'mp'=8] {'dp','ctx'}, use_global_device_ids=true, to_apply=%region_8.9 | all-reduce | flops 2048 | bytes 16384 | tf_op jit(solution)/shard_map/psum | solution.py:94
  504.6 0.6 fusion.34
  505.2 0.1 slice_convert_fusion
  505.3 0.2 copy.56
  505.5 0.2 copy.44
  505.7 0.1 constant_dynamic-slice_fusion.1
  505.7 0.1 fusion.22
  505.9 18.1 %while.14 = (s32[]{:T(128)}, f32[1,16,64,128]{3,2,1,0:T(8,128)S(1)}, s32[]{:T(128)}, bf16[16,1,16]{2,1,0:T(2,128)(2,1)S(1)}, bf16[16,1,16,64,128]{4,3,2,1,0:T(8,128)(2,1)}, /*index=5*/s32[]{:T(128)}, s32[]{:T(128)}) while((s32[]{:T(128)}, f32[1,16,64,128]{3,2,1,0:T(8,128)S(1)}, s32[]{:T(128)}, bf16[16,1,16]{2,1,0:T(2,128)(2,1)S(1)}, ...), condition=%wide.region_2.0_spmd.clone, body=%wide.region_1.0_spmd.clone.sunk | while | flops 655380 | bytes 1310985 | solution.py:39
  505.9 1.1 fusion.65
  507.1 1.1 fusion.65
  508.2 1.1 fusion.65
  509.3 1.1 fusion.65
  510.5 1.1 fusion.65
  511.6 1.1 fusion.65
  512.7 1.1 fusion.65
  513.8 1.1 fusion.65
  515.0 1.1 fusion.65
  516.1 1.1 fusion.65
  517.2 1.1 fusion.65
  518.4 1.1 fusion.65
  519.5 1.1 fusion.65
  520.6 1.1 fusion.65
  521.8 1.1 fusion.65
  522.9 1.1 fusion.65
  524.0 0.4 fusion.7
  524.4 0.6 multiply_reduce_fusion
  525.0 0.2 multiply_convert_fusion.4
  525.2 0.9 copy.57
  (49 shorter events, 0.5 us)
Async XLA Ops:
  7.2 3.2 copy-start.1
  7.2 147.1 %all-gather.10.cloned.1.call-start = ((), (), s32[]{:S(2)}) async-start(), calls=%async_computation.1 | async-start | bytes 1064960 | tf_op jit(solution)/shard_map/all_gather | solution.py:98
  7.9 302.7 %all-gather.8.cloned.1.call-start = ((), (), s32[]{:S(2)}) async-start(), calls=%async_computation | async-start | bytes 8519680 | tf_op jit(solution)/shard_map/all_gather | solution.py:97
  8.7 497.2 %all-gather.12.cloned.1.call-start = ((), (), s32[]{:S(2)}) async-start(), calls=%async_computation.2 | async-start | bytes 4456448 | tf_op jit(solution)/shard_map/all_gather | solution.py:22
  100.3 3.6 copy-start.5
  100.3 3.6 copy-start.4
  100.3 4.0 copy-start
  100.3 4.1 copy-start.3
  315.3 5.1 collective-permute-start
  320.8 13.4 %copy-start.2 = (f32[1024]{0:T(1024)S(1)}, f32[1024]{0:T(1024)}, u32[]{:S(2)}) copy-start(f32[1024]{0:T(1024)} %param.21) | copy-start | bytes 12292
  505.9 18.5 %copy-start.6 = (f32[16]{0:T(128)S(1)}, f32[16]{0:T(128)}, u32[]{:S(2)}) copy-start(f32[16]{0:T(128)} %param.20) | copy-start | bytes 196
Sparse Core Ops, SparseCore 0:
  10.9 143.2 all-gather.9
  157.2 153.3 all-gather.7
  334.2 75.3 all-gather.11
where the time goes:
time: 533 us
  blocking collectives  271 us (51%)
  waiting for transfers between devices  207 us (39%)
  other arithmetic  19.7 us (4%)
  between operations  14.1 us (3%)
  matrix products  12.9 us (2%)
    all_gather x1, waiting for transfers between devices, shards(): lax.all_gather(x_weight, ('dp', 'ctx'), axis=0, tiled=True)  155 us
    psum x1, blocking collectives, shards(): totals = lax.psum(powers, ('dp', 'ctx'))  141 us
    all_gather x1, blocking collectives, shards(): lax.all_gather(dt_weight, ('dp', 'ctx'), axis=0, tiled=True)  88.7 us
    all_gather x1, waiting for transfers between devices, shards(): lax.all_gather(bc_weight, ('dp', 'ctx'), axis=0, tiled=True)  49.7 us
    all_gather x1, blocking collectives, entering(): lax.all_gather(part.astype(kind), axis)  28.7 us
    select_n x16, other arithmetic, step(): return jax.tree.map(lambda a, b: jnp.where(reached, a, b), new, before)  17.5 us
    all_gather x1, blocking collectives, shards(): group_all = lax.all_gather(convolved[:, x_cols:], 'mp', axis=1, tiled=True)  11.9 us
  transfers between devices with their start and end apart: 4, of which 3 were waited for; matrix products, arithmetic and copies ran while one was open for 2% of the time, Pallas kernels for 0%

commit v1 on v0

--- a/solution.py
+++ b/solution.py
@@ -91,7 +91,7 @@
         ]
     )
     row_count = float(tok_rows * lax.axis_size("dp") * lax.axis_size("ctx"))
-    totals = lax.psum(powers, ("dp", "ctx"))
+    totals = lax.psum(lax.psum(powers, "dp"), "ctx")
     kurtosis = kurtosis_from(totals, row_count)
     panels = (
         lax.all_gather(x_weight, ("dp", "ctx"), axis=0, tiled=True),

time: 533 us -> 437 us (0.82)
  the two profiles are of different devices: /device:TPU:8 before, /device:TPU:2 now
where the time goes in v1:
time: 437 us; the launch traced here: 436 us
  waiting for transfers between devices  214 us (49%)
  blocking collectives  167 us (38%)
  other arithmetic  19.7 us (5%)
  between operations  14.1 us (3%)
  matrix products  12.9 us (3%)
    all_gather x1, waiting for transfers between devices, shards(): lax.all_gather(x_weight, ('dp', 'ctx'), axis=0, tiled=True)  154 us
    all_gather x1, blocking collectives, shards(): lax.all_gather(dt_weight, ('dp', 'ctx'), axis=0, tiled=True)  88.2 us
    all_gather x1, waiting for transfers between devices, shards(): lax.all_gather(bc_weight, ('dp', 'ctx'), axis=0, tiled=True)  49.3 us
    psum x2, blocking collectives, shards(): totals = lax.psum(lax.psum(powers, 'dp'), 'ctx')  37.9 us
    all_gather x1, blocking collectives, entering(): lax.all_gather(part.astype(kind), axis)  28.9 us
    select_n x16, other arithmetic, step(): return jax.tree.map(lambda a, b: jnp.where(reached, a, b), new, before)  17.5 us
    all_gather x1, blocking collectives, shards(): group_all = lax.all_gather(convolved[:, x_cols:], 'mp', axis=1, tiled=True)  12.2 us
  transfers between devices with their start and end apart: 4, of which 4 were waited for; matrix products, arithmetic and copies ran while one was open for 2% of the time, Pallas kernels for 0%

profile of v1, /device:TPU:2, one launch (start us, length us, event | category | flops | bytes accessed | tf_op | source)
XLA Modules:
  0.0 436.2 jit_solution(17702174703934169859)
XLA Ops:
  7.2 0.7 all-gather.10.cloned.1.call-update
  8.0 0.7 all-gather.8.cloned.1.call-update
  8.7 0.0 all-gather.12.cloned.1.call-start
  8.7 1.6 copy.40
  10.3 88.2 %all-gather.2 = bf16[64,64,16]{1,2,0:T(8,128)(2,1)S(1)} all-gather(bf16[1,64,16]{1,2,0:T(8,128)(2,1)S(1)} %bitcast.105), channel_id=1, replica_groups=mesh['dp'=4,'ctx'=16,'mp'=8] {'dp','ctx'}, dimensions={0}, use_global_device_ids=true | all-gather | bytes 133120 | tf_op jit(solution)/shard_map/all_gather | solution.py:99
  98.6 0.1 copy.47
  98.6 0.3 reshape.184
  98.9 0.9 convolution_bitcast_fusion
  99.9 3.3 multiply_convert_fusion
  103.2 0.2 convolution_convert_fusion.3
  103.5 0.1 broadcast_multiply_fusion
  103.5 0.1 copy.48
  103.6 0.2 reduce_window_sum.11
  103.8 0.1 copy.52
  103.9 0.1 fusion.54
  104.0 49.3 %all-gather.10.cloned.1.call-done = bf16[4096,128]{1,0:T(8,128)(2,1)} async-done(((bf16[64,128]{1,0:T(8,128)(2,1)}), bf16[4096,128]{1,0:T(8,128)(2,1)}) %all-gather.10.cloned.1.call-update) | async-done | bytes 1048592 | tf_op jit(solution)/shard_map/all_gather | solution.py:98
  153.3 1.7 convolution_convert_fusion.2
  155.0 154.5 %all-gather.8.cloned.1.call-done = bf16[4096,1024]{1,0:T(8,128)(2,1)} async-done(((bf16[64,1024]{1,0:T(8,128)(2,1)}), bf16[4096,1024]{1,0:T(8,128)(2,1)}) %all-gather.8.cloned.1.call-update) | async-done | bytes 8388624 | tf_op jit(solution)/shard_map/all_gather | solution.py:97
  309.5 4.7 %convolution_convert_fusion.1 = bf16[128,1024]{1,0:T(8,128)(2,1)S(1)} fusion(bf16[128,4096]{0,1:T(8,128)(2,1)S(1)} %bitcast.86, bf16[4096,1024]{1,0:T(8,128)(2,1)} %all-gather.8.cloned.1.call-done), kind=kOutput, calls=%fused_computation.13 | convolution fusion | flops 1073872896 | bytes 9699328 | tf_op jit(solution)/shard_map/dot_general | solution.py:102
  314.2 3.7 collective-permute-start
  317.8 0.1 slice_reduce_fusion.4
  318.0 0.2 copy.53
  318.2 1.0 collective-permute-done
  319.2 0.1 maximum_maximum_fusion
  319.3 0.4 multiply_convert_fusion.2
  319.7 12.2 %all_gather.26 = bf16[128,1024]{1,0:T(8,128)(2,1)S(1)} all-gather(bf16[128,128]{1,0:T(8,128)(2,1)S(1)} %slice.84), channel_id=1, replica_groups=mesh['dp'=4,'ctx'=16,'mp'=8] {'mp'}, dimensions={1}, use_global_device_ids=true | all-gather | bytes 294912 | tf_op jit(solution)/shard_map/all_gather | solution.py:118
  332.0 0.2 copy.54
  332.2 0.1 constant_dynamic-slice_fusion
  332.3 0.9 convolution_convert_fusion
  333.3 0.1 copy.51
  333.3 0.1 copy.49
  333.4 0.1 mul.262
  333.5 28.9 %all-gather.3 = bf16[16,1,16]{2,1,0:T(2,128)(2,1)S(1)} all-gather(bf16[1,1,16]{2,1,0:T(2,128)(2,1)S(1)} %get-tuple-element.160), channel_id=2, replica_groups=mesh['dp'=4,'ctx'=16,'mp'=8] {'ctx'}, dimensions={0}, use_global_device_ids=true | all-gather | bytes 544 | tf_op jit(solution)/shard_map/all_gather | solution.py:22
  362.4 0.3 convert_reduce_fusion
  362.7 9.4 %psum.14 = f32[4,512]{1,0:T(4,128)S(1)} all-reduce(f32[4,512]{1,0:T(4,128)S(1)} %pad_maximum_fusion.1), channel_id=1, replica_groups=mesh['dp'=4,'ctx'=16,'mp'=8] {'dp'}, use_global_device_ids=true, to_apply=%region_8.9 | all-reduce | flops 2048 | bytes 16384 | tf_op jit(solution)/shard_map/psum | solution.py:94
  372.1 28.5 %psum.15 = f32[4,512]{1,0:T(4,128)S(1)} all-reduce(f32[4,512]{1,0:T(4,128)S(1)} %psum.14), channel_id=1, replica_groups=mesh['dp'=4,'ctx'=16,'mp'=8] {'ctx'}, use_global_device_ids=true, to_apply=%region_9.10 | all-reduce | flops 2048 | bytes 16384 | tf_op jit(solution)/shard_map/psum | solution.py:94
  400.7 0.6 fusion.34
  401.3 0.1 slice_convert_fusion
  401.4 0.2 copy.56
  401.6 0.2 copy.44
  401.8 0.1 constant_dynamic-slice_fusion.1
  401.9 0.1 fusion.22
  402.0 7.5 %all-gather.12.cloned.1.call-done = bf16[256,64,128]{2,1,0:T(8,128)(2,1)} async-done(((bf16[16,64,128]{2,1,0:T(8,128)(2,1)}), bf16[256,64,128]{2,1,0:T(8,128)(2,1)}) %all-gather.12.cloned.1.call-update) | async-done | bytes 4194320 | tf_op jit(solution)/shard_map/all_gather | solution.py:22
  409.5 18.1 %while.14 = (s32[]{:T(128)}, f32[1,16,64,128]{3,2,1,0:T(8,128)S(1)}, s32[]{:T(128)}, bf16[16,1,16]{2,1,0:T(2,128)(2,1)S(1)}, bf16[16,1,16,64,128]{4,3,2,1,0:T(8,128)(2,1)}, /*index=5*/s32[]{:T(128)}, s32[]{:T(128)}) while((s32[]{:T(128)}, f32[1,16,64,128]{3,2,1,0:T(8,128)S(1)}, s32[]{:T(128)}, bf16[16,1,16]{2,1,0:T(2,128)(2,1)S(1)}, ...), condition=%wide.region_2.0_spmd.clone, body=%wide.region_1.0_spmd.clone.sunk | while | flops 655380 | bytes 1310985 | solution.py:39
  409.5 1.1 fusion.65
  410.6 1.1 fusion.65
  411.8 1.1 fusion.65
  412.9 1.1 fusion.65
  414.0 1.1 fusion.65
  415.2 1.1 fusion.65
  416.3 1.1 fusion.65
  417.4 1.1 fusion.65
  418.5 1.1 fusion.65
  419.7 1.1 fusion.65
  420.8 1.1 fusion.65
  421.9 1.1 fusion.65
  423.1 1.1 fusion.65
  424.2 1.1 fusion.65
  425.3 1.1 fusion.65
  426.5 1.1 fusion.65
  427.6 0.4 fusion.7
  428.0 0.6 multiply_reduce_fusion
  428.6 0.2 multiply_convert_fusion.4
  428.8 0.9 copy.57
  (50 shorter events, 0.6 us)
Async XLA Ops:
  7.2 3.2 copy-start.1
  7.2 146.1 %all-gather.10.cloned.1.call-start = ((), (), s32[]{:S(2)}) async-start(), calls=%async_computation.1 | async-start | bytes 1064960 | tf_op jit(solution)/shard_map/all_gather | solution.py:98
  7.9 301.6 %all-gather.8.cloned.1.call-start = ((), (), s32[]{:S(2)}) async-start(), calls=%async_computation | async-start | bytes 8519680 | tf_op jit(solution)/shard_map/all_gather | solution.py:97
  8.7 400.8 %all-gather.12.cloned.1.call-start = ((), (), s32[]{:S(2)}) async-start(), calls=%async_computation.2 | async-start | bytes 4456448 | tf_op jit(solution)/shard_map/all_gather | solution.py:22
  99.8 3.6 copy-start.5
  99.8 3.6 copy-start.4
  99.8 4.0 copy-start
  99.8 4.1 copy-start.3
  314.2 5.0 %collective-permute-start = (bf16[3,1152]{1,0:T(4,128)(2,1)S(1)}, bf16[3,1152]{1,0:T(4,128)(2,1)S(1)}, u32[]{:S(2)}, u32[]{:S(2)}) collective-permute-start(bf16[3,1152]{1,0:T(4,128)(2,1)S(1)} %fusion.32), channel_id=1, source_target_pairs={{0,8},{8,16},{16,24},{24,32},{32,40},{40,48},{48,56},{56,64},{64,7... | collective-permute-start | bytes 20744 | tf_op jit(solution)/shard_map/ppermute | solution.py:16
  319.7 13.7 %copy-start.2 = (f32[1024]{0:T(1024)S(1)}, f32[1024]{0:T(1024)}, u32[]{:S(2)}) copy-start(f32[1024]{0:T(1024)} %param.21) | copy-start | bytes 12292
  409.5 18.5 %copy-start.6 = (f32[16]{0:T(128)S(1)}, f32[16]{0:T(128)}, u32[]{:S(2)}) copy-start(f32[16]{0:T(128)} %param.20) | copy-start | bytes 196
Sparse Core Ops, SparseCore 0:
  10.9 142.3 all-gather.9
  156.3 153.1 all-gather.7
  333.4 76.0 all-gather.11
